TPU v7x, 128 devices: a whole 4x4x4 slice. The times are simulated.
128 devices in a mesh: ctx: 16 (over z, x_lo, core), head: 8 (over y, x_hi).
Axes of the slice: x: 4 (x_hi: 2, x_lo: 2; x = x_hi * 2 + x_lo), y: 4, z: 4, core: 2. Of those that a mesh axis runs over, the one named last changes fastest.
Arguments:
- queries: bfloat16 [24576, 3072], P('ctx', 'head'), may hold values from -160 to 160
- key_states: bfloat16 [24576, 3072], P('ctx', 'head'), may hold values from -12 to 12
- value_states: bfloat16 [24576, 3072], P('ctx', 'head'), may hold values from -18 to 18
- out_grads: bfloat16 [24576, 3072], P(('ctx', 'head')), may hold values from -6 to 6
- pattern: int32 [64, 8], replicated, may hold values from -1 to 63, as said below
Outputs:
- attended: bfloat16 [24576, 3072], P(('ctx', 'head'))
- query_grads: bfloat16 [24576, 3072], P('ctx', 'head')
- key_grads: bfloat16 [24576, 3072], P('ctx', 'head')
- value_grads: bfloat16 [24576, 3072], P('ctx', 'head')
Inputs may be any that keep to these rules, and one draw needn't show every extreme that they name: `pattern`: row t lists distinct tiles whose frame tile (tile // 4) differs from that of t by at most one; t itself is always listed; -1 marks an empty slot and empty slots come last; three or more tiles are listed in every row.
All inputs are finite; a program needn't handle non-finite values.
Results may differ from a plain program's by a relative error of at most 0.035.
Values may be sent and summed in bfloat16 or wider, within the bound.
No kernel may reach another device: no remote copies, remote signals or barrier semaphores. Data moves between devices by JAX's collectives and lax.ppermute only.
A program may use at most 256 MiB of HBM per device.

v0:
```python
import functools
import math

import jax
import jax.numpy as jnp
from jax import lax
from jax.experimental import pallas as pl
from jax.experimental.pallas import tpu as pltpu
from jax.sharding import PartitionSpec as P

HD = 128
TILE = 384
SPT = 4
KSLOT = 8
SCALE = 1.0 / math.sqrt(HD)
NT = (((1,), (1,)), ((), ()))
TN = (((0,), (0,)), ((), ()))


def with_halo(block, axis, dim):
    count = lax.axis_size(axis)
    forward = [(i, i + 1) for i in range(count - 1)]
    backward = [(target, source) for source, target in forward]
    low = lax.ppermute(block, axis, forward)
    high = lax.ppermute(block, axis, backward)
    return jnp.concatenate([low, block, high], axis=dim)


def from_behind(block, axis, distance):
    devices = range(lax.axis_size(axis))
    route = [(i - distance, i) for i in devices if i - distance in devices]
    return lax.ppermute(block, axis, route)


def lane_fold(x, op):
    parts = [x[:, j * HD : (j + 1) * HD] for j in range(x.shape[1] // HD)]
    return functools.reduce(op, parts)


def slot_rows(slots_ref, a, s):
    start = pl.multiple_of(slots_ref[a * KSLOT + s] * TILE, TILE)
    return pl.ds(start, TILE)


def forward_kernel(slots_ref, counts_ref, q_ref, k_ref, v_ref, o_ref, lse_ref, s_scr):
    a = pl.program_id(1)
    q = q_ref[...]
    count = counts_ref[a]
    rows = functools.partial(slot_rows, slots_ref, a)

    def score_pass(s, row_max):
        scores = lax.dot_general(
            q, k_ref[rows(s), :], NT, preferred_element_type=jnp.float32
        ) * SCALE
        s_scr[s] = scores
        return jnp.maximum(row_max, lane_fold(scores, jnp.maximum))

    row_max = lax.fori_loop(
        0, count, score_pass, jnp.full((TILE, HD), -jnp.inf, jnp.float32)
    )
    row_max = jnp.max(row_max, axis=1, keepdims=True)

    def exp_pass(s, carry):
        row_total, acc = carry
        e = jnp.exp(s_scr[s] - row_max)
        acc = acc + jnp.dot(
            e.astype(jnp.bfloat16), v_ref[rows(s), :], preferred_element_type=jnp.float32
        )
        return row_total + lane_fold(e, jnp.add), acc

    row_total, acc = lax.fori_loop(
        0, count, exp_pass,
        (jnp.zeros((TILE, HD), jnp.float32), jnp.zeros((TILE, HD), jnp.float32)),
    )
    row_total = jnp.sum(row_total, axis=1, keepdims=True)
    o_ref[...] = (acc * (1.0 / row_total)).astype(jnp.bfloat16)
    lse_ref[...] = jnp.broadcast_to(row_max + jnp.log(row_total), (TILE, HD))


def backward_kernel(
    slots_ref, counts_ref, q_ref, do_ref, o_ref, lse_ref, k_ref, v_ref,
    dq_ref, dk_ref, dv_ref,
):
    a = pl.program_id(1)

    @pl.when(a == 0)
    def _():
        dk_ref[...] = jnp.zeros_like(dk_ref)
        dv_ref[...] = jnp.zeros_like(dv_ref)

    q = q_ref[...]
    do = do_ref[...]
    lse = lse_ref[:, :1]
    delta = jnp.sum(
        do.astype(jnp.float32) * o_ref[...].astype(jnp.float32), axis=1, keepdims=True
    )
    count = counts_ref[a]
    rows = functools.partial(slot_rows, slots_ref, a)

    def grad_pass(s, dq_acc):
        r = rows(s)
        k = k_ref[r, :]
        scores = lax.dot_general(q, k, NT, preferred_element_type=jnp.float32) * SCALE
        w = jnp.exp(scores - lse)
        g = lax.dot_general(do, v_ref[r, :], NT, preferred_element_type=jnp.float32)
        ds = (w * (g - delta)).astype(jnp.bfloat16)
        dk_ref[r, :] += lax.dot_general(ds, q, TN, preferred_element_type=jnp.float32)
        dv_ref[r, :] += lax.dot_general(
            w.astype(jnp.bfloat16), do, TN, preferred_element_type=jnp.float32
        )
        return dq_acc + jnp.dot(ds, k, preferred_element_type=jnp.float32)

    dq = lax.fori_loop(0, count, grad_pass, jnp.zeros((TILE, HD), jnp.float32))
    dq_ref[...] = (dq * SCALE).astype(jnp.bfloat16)


def specs(row_count, ext_rows):
    tile_spec = pl.BlockSpec((TILE, HD), lambda h, a, sl, ct: (a, h))
    ext_spec = pl.BlockSpec((ext_rows, HD), lambda h, a, sl, ct: (0, h))
    return tile_spec, ext_spec


def attention_forward(slots, counts, queries, keys, values):
    row_count, col_count = queries.shape
    tile_spec, ext_spec = specs(row_count, keys.shape[0])
    return pl.pallas_call(
        forward_kernel,
        grid_spec=pltpu.PrefetchScalarGridSpec(
            num_scalar_prefetch=2,
            grid=(col_count // HD, row_count // TILE),
            in_specs=[tile_spec, ext_spec, ext_spec],
            out_specs=[tile_spec, tile_spec],
            scratch_shapes=[pltpu.VMEM((KSLOT, TILE, TILE), jnp.float32)],
        ),
        out_shape=[
            jax.ShapeDtypeStruct((row_count, col_count), jnp.bfloat16),
            jax.ShapeDtypeStruct((row_count, col_count), jnp.float32),
        ],
        compiler_params=pltpu.CompilerParams(
            dimension_semantics=("arbitrary", "arbitrary"),
            vmem_limit_bytes=48 * 1024 * 1024,
        ),
    )(slots, counts, queries, keys, values)


def attention_backward(slots, counts, queries, grads, out, lse, keys, values):
    row_count, col_count = queries.shape
    ext_rows = keys.shape[0]
    tile_spec, ext_spec = specs(row_count, ext_rows)
    return pl.pallas_call(
        backward_kernel,
        grid_spec=pltpu.PrefetchScalarGridSpec(
            num_scalar_prefetch=2,
            grid=(col_count // HD, row_count // TILE),
            in_specs=[tile_spec, tile_spec, tile_spec, tile_spec, ext_spec, ext_spec],
            out_specs=[tile_spec, ext_spec, ext_spec],
        ),
        out_shape=[
            jax.ShapeDtypeStruct((row_count, col_count), jnp.bfloat16),
            jax.ShapeDtypeStruct((ext_rows, col_count), jnp.float32),
            jax.ShapeDtypeStruct((ext_rows, col_count), jnp.float32),
        ],
        compiler_params=pltpu.CompilerParams(
            dimension_semantics=("arbitrary", "arbitrary"),
            vmem_limit_bytes=48 * 1024 * 1024,
        ),
    )(slots, counts, queries, grads, out, lse, keys, values)


def shards(queries, key_states, value_states, out_grads, pattern):
    row_count, col_count = queries.shape
    own_tiles = row_count // TILE
    first_tile = lax.axis_index("ctx") * own_tiles
    base_tile = first_tile - SPT
    rims = with_halo(jnp.stack((key_states, value_states)), "ctx", 1)
    grads_heads = lax.all_to_all(out_grads, "head", split_axis=1, concat_axis=0, tiled=True)
    listed = lax.dynamic_slice_in_dim(pattern, first_tile, own_tiles, 0)
    allowed = listed >= 0
    slots = jnp.where(allowed, listed - base_tile, 0).reshape(-1).astype(jnp.int32)
    counts = jnp.sum(allowed.astype(jnp.int32), axis=1)
    out, lse = attention_forward(slots, counts, queries, rims[0], rims[1])
    attended = lax.all_to_all(out, "head", split_axis=0, concat_axis=1, tiled=True)
    dq, dk, dv = attention_backward(
        slots, counts, queries, grads_heads, out, lse, rims[0], rims[1]
    )
    parts = jnp.stack((dk, dv))
    own_part = parts[:, row_count : 2 * row_count]
    lower_part = parts[:, :row_count].astype(jnp.bfloat16)
    upper_part = parts[:, 2 * row_count :].astype(jnp.bfloat16)
    from_above = from_behind(lower_part, "ctx", -1).astype(jnp.float32)
    from_below = from_behind(upper_part, "ctx", 1).astype(jnp.float32)
    total = own_part + from_above + from_below
    key_grads = (total[0] * SCALE).astype(jnp.bfloat16)
    value_grads = total[1].astype(jnp.bfloat16)
    return (attended, dq, key_grads, value_grads)


def solution(mesh):
    return jax.shard_map(
        shards,
        mesh=mesh,
        in_specs=(
            P("ctx", "head"),
            P("ctx", "head"),
            P("ctx", "head"),
            P(("ctx", "head"), None),
            P(),
        ),
        out_specs=(P(("ctx", "head"), None), P("ctx", "head"), P("ctx", "head"), P("ctx", "head")),
        check_vma=False,
    )
```

profile of v0, /device:TPU:33, one launch (start us, length us, event | category | flops | bytes accessed | tf_op | source)
XLA Modules:
  0.0 284.0 jit_solution(7802760353154673784)
XLA Ops:
  0.6 0.0 copy-start.5
  0.6 3.4 %pad_maximum_fusion.2 = bf16[2,1536,384]{2,1,0:T(8,128)(2,1)} fusion(bf16[1,1536,384]{2,1,0:T(8,128)(2,1)} %bitcast.29, bf16[1,1536,384]{2,1,0:T(8,128)(2,1)} %bitcast.31), kind=kLoop, calls=%fused_computation.13 | loop fusion | flops 1179648 | bytes 4718592 | tf_op jit(solution)/shard_map/stack | solution.py:175
  4.1 3.8 %collective-permute-start = (bf16[2,1536,384]{2,1,0:T(8,128)(2,1)}, bf16[2,1536,384]{2,1,0:T(8,128)(2,1)}, u32[]{:S(2)}, u32[]{:S(2)}) collective-permute-start(bf16[2,1536,384]{2,1,0:T(8,128)(2,1)} %pad_maximum_fusion.2), channel_id=1, source_target_pairs={{0,8},{8,16},{16,24},{24,32},{32,40},{40,48},{48,56},{56,64},{64,7... | collective-permute-start | bytes 7077896 | tf_op jit(solution)/shard_map/ppermute | solution.py:24
  7.9 1.9 collective-permute-start.1
  9.8 1.1 copy.15
  10.9 6.4 %all-to-all-start.1 = ((bf16[192,8,384]{2,0,1:T(8,128)(2,1)}), bf16[192,8,384]{2,0,1:T(8,128)(2,1)S(1)}, u32[]{:S(2)}, u32[]{:S(2)}) async-start(bf16[192,8,384]{2,0,1:T(8,128)(2,1)} %bitcast.33), calls=%async_computation.1 | async-start | bytes 2359296 | tf_op jit(solution)/shard_map/all_to_all | solution.py:176
  17.3 0.0 copy-done.6
  17.3 0.1 convert_reduce_fusion
  17.4 0.1 subtract_select_fusion
  17.5 0.1 copy.9
  17.6 0.1 reshape.21.slots_ref
  17.7 37.9 %collective-permute-done = bf16[2,1536,384]{2,1,0:T(8,128)(2,1)} collective-permute-done((bf16[2,1536,384]{2,1,0:T(8,128)(2,1)}, bf16[2,1536,384]{2,1,0:T(8,128)(2,1)}, u32[]{:S(2)}, u32[]{:S(2)}) %collective-permute-start) | collective-permute-done | bytes 2359328 | tf_op jit(solution)/shard_map/ppermute | solution.py:24
  55.6 8.0 %collective-permute-done.1 = bf16[2,1536,384]{2,1,0:T(8,128)(2,1)} collective-permute-done((bf16[2,1536,384]{2,1,0:T(8,128)(2,1)}, bf16[2,1536,384]{2,1,0:T(8,128)(2,1)}, u32[]{:S(2)}, u32[]{:S(2)}) %collective-permute-start.1) | collective-permute-done | bytes 2359328 | tf_op jit(solution)/shard_map/ppermute | solution.py:25
  63.6 3.6 %pad_maximum_fusion.1 = bf16[2,4608,384]{2,1,0:T(8,128)(2,1)S(1)} fusion(bf16[2,1536,384]{2,1,0:T(8,128)(2,1)} %collective-permute-done.1, bf16[1,1536,384]{2,1,0:T(8,128)(2,1)S(1)} %bitcast.30, bf16[1,1536,384]{2,1,0:T(8,128)(2,1)S(1)} %bitcast.32, bf16[2,1536,384]{2,1,0:T(8,128)(2,1)} %collective-permute-done), kind=kLoop, calls=%fused_computation.4 | loop fusion | flops 28311552 | bytes 14155776 | tf_op jit(solution)/shard_map/concatenate | solution.py:26
  67.2 0.0 copy-start
  67.2 3.5 %slice_bitcast_fusion = (bf16[4608,384]{1,0:T(8,128)(2,1)}, bf16[4608,384]{1,0:T(8,128)(2,1)}) fusion(bf16[2,4608,384]{2,1,0:T(8,128)(2,1)S(1)} %pad_maximum_fusion.1), kind=kLoop, calls=%fused_computation.8 | loop fusion | bytes 14155776 | tf_op jit(solution)/shard_map/squeeze | solution.py:181
  70.8 55.5 %shard_map.84 = (bf16[1536,384]{1,0:T(8,128)(2,1)S(1)}, f32[1536,384]{1,0:T(8,128)S(1)}) custom-call(s32[32]{0:T(128)S(1)} %reshape.21.slots_ref, s32[4]{0:T(128)S(1)} %get-tuple-element.14.counts_ref, bf16[1536,384]{1,0:T(8,128)(2,1)S(1)} %copy-done, bf16[4608,384]{1,0:T(8,128)(2,1)} %get-tuple-element.19.k_ref, bf16[4608,384]{1,0:T(8,128)(2,1)} %get-tuple-element.18.v_ref), custom_call_target="tpu_custom_call" | custom-call | tf_op jit(solution)/shard_map/pallas_call | solution.py:126
  126.3 1.4 copy-done.1
  127.7 0.0 all-to-all-done.1
  127.7 1.7 copy-done.2
  129.4 72.8 %shard_map.85 = (bf16[1536,384]{1,0:T(8,128)(2,1)}, f32[4608,384]{1,0:T(8,128)}, f32[4608,384]{1,0:T(8,128)}) custom-call(s32[32]{0:T(128)S(1)} %reshape.21.slots_ref, s32[4]{0:T(128)S(1)} %get-tuple-element.14.counts_ref, bf16[1536,384]{1,0:T(8,128)(2,1)S(1)} %copy-done, bf16[1536,384]{1,0:T(8,128)(2,1)S(1)} %bitcast.23, ...), custom_call_target="tpu_custom_call" | custom-call | tf_op jit(solution)/shard_map/pallas_call | solution.py:150
  202.2 8.8 %fusion = bf16[2,4608,384]{2,1,0:T(8,128)(2,1)} fusion(f32[1,4608,384]{2,1,0:T(8,128)} %bitcast.27, f32[1,4608,384]{2,1,0:T(8,128)} %bitcast.25), kind=kLoop, calls=%fused_computation.3 | loop fusion | flops 3538944 | bytes 21233664 | tf_op jit(solution)/shard_map/convert.2
  211.0 2.8 %fusion.7 = (bf16[2,1536,384]{2,1,0:T(8,128)(2,1)S(1)}, bf16[2,1536,384]{2,1,0:T(8,128)(2,1)S(1)}) fusion(bf16[2,4608,384]{2,1,0:T(8,128)(2,1)} %fusion), kind=kLoop, calls=%fused_computation.20 | loop fusion | bytes 9437184 | tf_op jit(solution)/shard_map/slice | solution.py:188
  213.9 1.9 collective-permute-start.2
  215.8 3.6 %collective-permute-start.3 = (bf16[2,1536,384]{2,1,0:T(8,128)(2,1)S(1)}, bf16[2,1536,384]{2,1,0:T(8,128)(2,1)S(1)}, u32[]{:S(2)}, u32[]{:S(2)}) collective-permute-start(bf16[2,1536,384]{2,1,0:T(8,128)(2,1)S(1)} %get-tuple-element.17), channel_id=1, source_target_pairs={{0,8},{8,16},{16,24},{24,32},{32,40},{40,48},{48,56},{56,64},{64,7... | collective-permute-start | bytes 7077896 | tf_op jit(solution)/shard_map/ppermute | solution.py:32
  219.5 57.7 %all_to_all.38 = bf16[8,192,384]{2,1,0:T(8,128)(2,1)S(1)} all-to-all(bf16[8,192,384]{2,1,0:T(8,128)(2,1)S(1)} %bitcast.24), channel_id=1, replica_groups=mesh['ctx'=16,'head'=8] {'head'}, dimensions={0} | all-to-all | bytes 2359296 | tf_op jit(solution)/shard_map/all_to_all | solution.py:182
  277.1 1.2 copy.13
  278.4 0.0 collective-permute-done.2
  278.4 0.0 collective-permute-done.3
  278.4 3.2 %fusion.3 = f32[2,1536,384]{2,1,0:T(8,128)S(1)} fusion(f32[1,4608,384]{2,1,0:T(8,128)} %bitcast.26, f32[1,4608,384]{2,1,0:T(8,128)} %bitcast.28, bf16[2,1536,384]{2,1,0:T(8,128)(2,1)S(1)} %collective-permute-done.3, bf16[2,1536,384]{2,1,0:T(8,128)(2,1)S(1)} %collective-permute-done.2), kind=kLoop, calls=%fused_computation.7 | loop fusion | flops 5898240 | bytes 23592960 | tf_op jit(solution)/shard_map/add | solution.py:192
  281.6 1.3 fusion.5
  282.9 1.1 fusion.6
  (9 shorter events, 0.0 us)
Async XLA Ops:
  0.6 9.2 %copy-start.5 = (bf16[192,3072]{1,0:T(8,128)(2,1)S(1)}, bf16[192,3072]{1,0:T(8,128)(2,1)}, u32[]{:S(2)}) copy-start(bf16[192,3072]{1,0:T(8,128)(2,1)} %param.8) | copy-start | bytes 3538948
  4.1 13.3 %copy-start.6 = (s32[64,8]{0,1:T(8,128)S(1)}, s32[64,8]{0,1:T(8,128)}, u32[]{:S(2)}) copy-start(s32[64,8]{0,1:T(8,128)} %param.9) | copy-start | bytes 6148
  4.1 59.6 %copy-start.3 = (bf16[1536,384]{1,0:T(8,128)(2,1)S(1)}, bf16[1536,384]{1,0:T(8,128)(2,1)}, u32[]{:S(2)}) copy-start(bf16[1536,384]{1,0:T(8,128)(2,1)} %param.7) | copy-start | bytes 3538948
  4.1 59.6 %copy-start.4 = (bf16[1536,384]{1,0:T(8,128)(2,1)S(1)}, bf16[1536,384]{1,0:T(8,128)(2,1)}, u32[]{:S(2)}) copy-start(bf16[1536,384]{1,0:T(8,128)(2,1)} %param.6) | copy-start | bytes 3538948
  4.1 51.5 %collective-permute-start = (bf16[2,1536,384]{2,1,0:T(8,128)(2,1)}, bf16[2,1536,384]{2,1,0:T(8,128)(2,1)}, u32[]{:S(2)}, u32[]{:S(2)}) collective-permute-start(bf16[2,1536,384]{2,1,0:T(8,128)(2,1)} %pad_maximum_fusion.2), channel_id=1, source_target_pairs={{0,8},{8,16},{16,24},{24,32},{32,40},{40,48},{48,56},{56,64},{64,7... | collective-permute-start | bytes 7077896 | tf_op jit(solution)/shard_map/ppermute | solution.py:24
  7.9 55.8 %collective-permute-start.1 = (bf16[2,1536,384]{2,1,0:T(8,128)(2,1)}, bf16[2,1536,384]{2,1,0:T(8,128)(2,1)}, u32[]{:S(2)}, u32[]{:S(2)}) collective-permute-start(bf16[2,1536,384]{2,1,0:T(8,128)(2,1)} %pad_maximum_fusion.2), channel_id=1, source_target_pairs={{8,0},{16,8},{24,16},{32,24},{40,32},{48,40},{56,48},{64,56},{72,6... | collective-permute-start | bytes 7077896 | tf_op jit(solution)/shard_map/ppermute | solution.py:25
  10.9 116.8 %all-to-all-start.1 = ((bf16[192,8,384]{2,0,1:T(8,128)(2,1)}), bf16[192,8,384]{2,0,1:T(8,128)(2,1)S(1)}, u32[]{:S(2)}, u32[]{:S(2)}) async-start(bf16[192,8,384]{2,0,1:T(8,128)(2,1)} %bitcast.33), calls=%async_computation.1 | async-start | bytes 2359296 | tf_op jit(solution)/shard_map/all_to_all | solution.py:176
  67.2 3.5 %copy-start = (bf16[1536,384]{1,0:T(8,128)(2,1)S(1)}, bf16[1536,384]{1,0:T(8,128)(2,1)}, u32[]{:S(2)}) copy-start(bf16[1536,384]{1,0:T(8,128)(2,1)} %q_ref.3) | copy-start | bytes 3538948
  126.3 1.4 copy-start.1
  127.7 1.7 copy-start.2
  213.9 64.5 %collective-permute-start.2 = (bf16[2,1536,384]{2,1,0:T(8,128)(2,1)S(1)}, bf16[2,1536,384]{2,1,0:T(8,128)(2,1)S(1)}, u32[]{:S(2)}, u32[]{:S(2)}) collective-permute-start(bf16[2,1536,384]{2,1,0:T(8,128)(2,1)S(1)} %get-tuple-element.16), channel_id=1, source_target_pairs={{8,0},{16,8},{24,16},{32,24},{40,32},{48,40},{56,48},{64,56},{72,6... | collective-permute-start | bytes 7077896 | tf_op jit(solution)/shard_map/ppermute | solution.py:32
  215.8 62.5 %collective-permute-start.3 = (bf16[2,1536,384]{2,1,0:T(8,128)(2,1)S(1)}, bf16[2,1536,384]{2,1,0:T(8,128)(2,1)S(1)}, u32[]{:S(2)}, u32[]{:S(2)}) collective-permute-start(bf16[2,1536,384]{2,1,0:T(8,128)(2,1)S(1)} %get-tuple-element.17), channel_id=1, source_target_pairs={{0,8},{8,16},{16,24},{24,32},{32,40},{40,48},{48,56},{56,64},{64,7... | collective-permute-start | bytes 7077896 | tf_op jit(solution)/shard_map/ppermute | solution.py:32
where the time goes:
time: 284 us
  Pallas kernels  128 us (45%)
  blocking collectives  57.7 us (20%)
  waiting for transfers between devices  46 us (16%)
  other arithmetic  20.5 us (7%)
  starting transfers between devices  17.6 us (6%)
  local copies, waits for them, and re-layouts  13.2 us (5%)
    pallas_call x1, Pallas kernels, attention_backward(): pl.pallas_call(backward_kernel, grid_spec=pltpu.PrefetchScalarGridSpec(nu...  72.8 us
    all_to_all x1, blocking collectives, shards(): lax.all_to_all(out, 'head', split_axis=0, concat_axis=1, tiled=True)  57.7 us
    pallas_call x1, Pallas kernels, attention_forward(): pl.pallas_call(forward_kernel, grid_spec=pltpu.PrefetchScalarGridSpec(num...  55.5 us
    ppermute x1, waiting for transfers between devices, with_halo(): low = lax.ppermute(block, axis, forward)  37.9 us
    another operation x1, other arithmetic  8.85 us
    ppermute x1, waiting for transfers between devices, with_halo(): high = lax.ppermute(block, axis, backward)  8.04 us
    all_to_all x1, starting transfers between devices, shards(): lax.all_to_all(out_grads, 'head', split_axis=1, concat_axis=0, tiled=True)  6.36 us
  transfers between devices with their start and end apart: 5, of which 2 were waited for; matrix products, arithmetic and copies ran while one was open for 3% of the time, Pallas kernels for 20%

commit v1 on v0

--- a/solution.py
+++ b/solution.py
@@ -77,41 +77,60 @@
     lse_ref[...] = jnp.broadcast_to(row_max + jnp.log(row_total), (TILE, HD))
 
 
-def backward_kernel(
-    slots_ref, counts_ref, q_ref, do_ref, o_ref, lse_ref, k_ref, v_ref,
-    dq_ref, dk_ref, dv_ref,
-):
-    a = pl.program_id(1)
-
-    @pl.when(a == 0)
-    def _():
-        dk_ref[...] = jnp.zeros_like(dk_ref)
-        dv_ref[...] = jnp.zeros_like(dv_ref)
-
-    q = q_ref[...]
-    do = do_ref[...]
-    lse = lse_ref[:, :1]
-    delta = jnp.sum(
-        do.astype(jnp.float32) * o_ref[...].astype(jnp.float32), axis=1, keepdims=True
-    )
-    count = counts_ref[a]
-    rows = functools.partial(slot_rows, slots_ref, a)
-
-    def grad_pass(s, dq_acc):
-        r = rows(s)
-        k = k_ref[r, :]
-        scores = lax.dot_general(q, k, NT, preferred_element_type=jnp.float32) * SCALE
-        w = jnp.exp(scores - lse)
-        g = lax.dot_general(do, v_ref[r, :], NT, preferred_element_type=jnp.float32)
-        ds = (w * (g - delta)).astype(jnp.bfloat16)
-        dk_ref[r, :] += lax.dot_general(ds, q, TN, preferred_element_type=jnp.float32)
-        dv_ref[r, :] += lax.dot_general(
-            w.astype(jnp.bfloat16), do, TN, preferred_element_type=jnp.float32
+def make_backward_kernel(own):
+    def backward_kernel(
+        slots_ref, counts_ref, q_ref, do_ref, o_ref, lse_ref, k_ref, v_ref, *rest
+    ):
+        if own:
+            dq_in_ref, dq_ref, dk_ref, dv_ref = rest
+        else:
+            dq_ref, dk_ref, dv_ref = rest
+        a = pl.program_id(1)
+
+        @pl.when(a == 0)
+        def _():
+            dk_ref[...] = jnp.zeros_like(dk_ref)
+            dv_ref[...] = jnp.zeros_like(dv_ref)
+
+        q = q_ref[...]
+        do = do_ref[...]
+        lse = lse_ref[:, :1]
+        delta = jnp.sum(
+            do.astype(jnp.float32) * o_ref[...].astype(jnp.float32), axis=1, keepdims=True
         )
-        return dq_acc + jnp.dot(ds, k, preferred_element_type=jnp.float32)
-
-    dq = lax.fori_loop(0, count, grad_pass, jnp.zeros((TILE, HD), jnp.float32))
-    dq_ref[...] = (dq * SCALE).astype(jnp.bfloat16)
+        count = counts_ref[a]
+        rows = functools.partial(slot_rows, slots_ref, a)
+
+        def acc_rows(s):
+            slot = slots_ref[a * KSLOT + s]
+            if own:
+                slot = slot - SPT
+            else:
+                slot = jnp.where(slot < SPT, slot, slot - SPT)
+            return pl.ds(pl.multiple_of(slot * TILE, TILE), TILE)
+
+        def grad_pass(s, dq_acc):
+            r = rows(s)
+            ar = acc_rows(s)
+            k = k_ref[r, :]
+            scores = lax.dot_general(q, k, NT, preferred_element_type=jnp.float32) * SCALE
+            w = jnp.exp(scores - lse)
+            g = lax.dot_general(do, v_ref[r, :], NT, preferred_element_type=jnp.float32)
+            ds = (w * (g - delta)).astype(jnp.bfloat16)
+            dk_ref[ar, :] += lax.dot_general(ds, q, TN, preferred_element_type=jnp.float32)
+            dv_ref[ar, :] += lax.dot_general(
+                w.astype(jnp.bfloat16), do, TN, preferred_element_type=jnp.float32
+            )
+            return dq_acc + jnp.dot(ds, k, preferred_element_type=jnp.float32)
+
+        init = dq_in_ref[...] if own else jnp.zeros((TILE, HD), jnp.float32)
+        dq = lax.fori_loop(0, count, grad_pass, init)
+        if own:
+            dq_ref[...] = (dq * SCALE).astype(jnp.bfloat16)
+        else:
+            dq_ref[...] = dq
+
+    return backward_kernel
 
 
 def specs(row_count, ext_rows):
@@ -143,28 +162,50 @@
     )(slots, counts, queries, keys, values)
 
 
-def attention_backward(slots, counts, queries, grads, out, lse, keys, values):
+def attention_backward(slots, counts, queries, grads, out, lse, keys, values, dq_in=None):
     row_count, col_count = queries.shape
     ext_rows = keys.shape[0]
+    own = dq_in is not None
+    acc_rows = row_count if own else ext_rows - row_count
     tile_spec, ext_spec = specs(row_count, ext_rows)
+    acc_spec = pl.BlockSpec((acc_rows, HD), lambda h, a, sl, ct: (0, h))
+    operands = [slots, counts, queries, grads, out, lse, keys, values]
+    in_specs = [tile_spec, tile_spec, tile_spec, tile_spec, ext_spec, ext_spec]
+    if own:
+        operands.append(dq_in)
+        in_specs.append(tile_spec)
+    dq_type = jnp.bfloat16 if own else jnp.float32
     return pl.pallas_call(
-        backward_kernel,
+        make_backward_kernel(own),
         grid_spec=pltpu.PrefetchScalarGridSpec(
             num_scalar_prefetch=2,
             grid=(col_count // HD, row_count // TILE),
-            in_specs=[tile_spec, tile_spec, tile_spec, tile_spec, ext_spec, ext_spec],
-            out_specs=[tile_spec, ext_spec, ext_spec],
+            in_specs=in_specs,
+            out_specs=[tile_spec, acc_spec, acc_spec],
         ),
         out_shape=[
-            jax.ShapeDtypeStruct((row_count, col_count), jnp.bfloat16),
-            jax.ShapeDtypeStruct((ext_rows, col_count), jnp.float32),
-            jax.ShapeDtypeStruct((ext_rows, col_count), jnp.float32),
+            jax.ShapeDtypeStruct((row_count, col_count), dq_type),
+            jax.ShapeDtypeStruct((acc_rows, col_count), jnp.float32),
+            jax.ShapeDtypeStruct((acc_rows, col_count), jnp.float32),
         ],
         compiler_params=pltpu.CompilerParams(
             dimension_semantics=("arbitrary", "arbitrary"),
             vmem_limit_bytes=48 * 1024 * 1024,
         ),
-    )(slots, counts, queries, grads, out, lse, keys, values)
+    )(*operands)
+
+
+def split_slots(listed, base_tile, first_tile, own_tiles):
+    allowed = listed >= 0
+    mine = allowed & (listed >= first_tile) & (listed < first_tile + own_tiles)
+    near = allowed & ~mine
+    slots = jnp.where(allowed, listed - base_tile, 0)
+    lists = []
+    for keep in (mine, near):
+        order = jnp.argsort(~keep, axis=1, stable=True)
+        picked = jnp.take_along_axis(slots, order, axis=1)
+        lists.append((picked.reshape(-1).astype(jnp.int32), jnp.sum(keep.astype(jnp.int32), axis=1)))
+    return lists
 
 
 def shards(queries, key_states, value_states, out_grads, pattern):
@@ -180,13 +221,19 @@
     counts = jnp.sum(allowed.astype(jnp.int32), axis=1)
     out, lse = attention_forward(slots, counts, queries, rims[0], rims[1])
     attended = lax.all_to_all(out, "head", split_axis=0, concat_axis=1, tiled=True)
-    dq, dk, dv = attention_backward(
-        slots, counts, queries, grads_heads, out, lse, rims[0], rims[1]
-    )
-    parts = jnp.stack((dk, dv))
-    own_part = parts[:, row_count : 2 * row_count]
-    lower_part = parts[:, :row_count].astype(jnp.bfloat16)
-    upper_part = parts[:, 2 * row_count :].astype(jnp.bfloat16)
+    (own_slots, own_counts), (near_slots, near_counts) = split_slots(
+        listed, base_tile, first_tile, own_tiles
+    )
+    dq_part, dk_near, dv_near = attention_backward(
+        near_slots, near_counts, queries, grads_heads, out, lse, rims[0], rims[1]
+    )
+    near = jnp.stack((dk_near, dv_near)).astype(jnp.bfloat16)
+    lower_part = near[:, :row_count]
+    upper_part = near[:, row_count:]
+    dq, dk_own, dv_own = attention_backward(
+        own_slots, own_counts, queries, grads_heads, out, lse, rims[0], rims[1], dq_part
+    )
+    own_part = jnp.stack((dk_own, dv_own))
     from_above = from_behind(lower_part, "ctx", -1).astype(jnp.float32)
     from_below = from_behind(upper_part, "ctx", 1).astype(jnp.float32)
     total = own_part + from_above + from_below

time: 284 us -> 257 us (0.905)
  blocking collectives: 57.7 us -> 0 us
  waiting for transfers between devices: 46 us -> 69.8 us
  Pallas kernels: 128 us -> 121 us
  starting transfers between devices: 17.6 us -> 24.4 us
  other arithmetic: 20.5 us -> 23.9 us
    all_to_all x1 -> x0, blocking collectives: 57.7 us -> none  [shards(): lax.all_to_all(out, 'head', split_axis=0, concat_axis=1, tiled=True)]
    all_to_all x0 -> x1, waiting for transfers between devices: none -> 25.8 us  [shards(): lax.all_to_all(out, 'head', split_axis=0, concat_axis=1, tiled=True)]
    all_to_all x0 -> x1, starting transfers between devices: none -> 6.66 us  [shards(): lax.all_to_all(out, 'head', split_axis=0, concat_axis=1, tiled=True)]
    pallas_call x1, Pallas kernels: 55.5 us -> 50.3 us  [attention_forward(): pl.pallas_call(forward_kernel, grid_spec=pltpu.PrefetchScalarGridSpec(num...]
    gather x0 -> x10, local copies, waits for them, and re-layouts: none -> 4.43 us  [split_slots(): picked = jnp.take_along_axis(slots, order, axis=1)]
    slice x1 -> x0, local copies, waits for them, and re-layouts: 2.85 us -> none  [shards(): lower_part = parts[:, :row_count].astype(jnp.bfloat16)]
    pallas_call x1 -> x2, Pallas kernels: 72.8 us -> 71 us  [attention_backward(): pl.pallas_call(make_backward_kernel(own), grid_spec=pltpu.PrefetchScalarG...]
    another operation x1 -> x2, other arithmetic: 8.85 us -> 7.55 us  [shards(): near = jnp.stack((dk_near, dv_near)).astype(jnp.bfloat16)]
  transfers between devices with their start and end apart: 5 -> 6, of which waited for: 2 -> 3; matrix products, arithmetic and copies ran while one was open for 3% -> 7% of each run, Pallas kernels for 20% -> 30%
where the time goes in v1:
time: 257 us; the launch traced here: 256 us
  Pallas kernels  121 us (47%)
  waiting for transfers between devices  69.8 us (27%)
  starting transfers between devices  24.4 us (9%)
  other arithmetic  23.9 us (9%)
  local copies, waits for them, and re-layouts  15.7 us (6%)
    pallas_call x2, Pallas kernels, attention_backward(): pl.pallas_call(make_backward_kernel(own), grid_spec=pltpu.PrefetchScalarG...  71 us
    pallas_call x1, Pallas kernels, attention_forward(): pl.pallas_call(forward_kernel, grid_spec=pltpu.PrefetchScalarGridSpec(num...  50.3 us
    ppermute x1, waiting for transfers between devices, with_halo(): low = lax.ppermute(block, axis, forward)  35.9 us
    all_to_all x1, waiting for transfers between devices, shards(): lax.all_to_all(out, 'head', split_axis=0, concat_axis=1, tiled=True)  25.8 us
    ppermute x1, waiting for transfers between devices, with_halo(): high = lax.ppermute(block, axis, backward)  8.04 us
    another operation x2, other arithmetic, shards(): near = jnp.stack((dk_near, dv_near)).astype(jnp.bfloat16)  7.55 us
    all_to_all x1, starting transfers between devices, shards(): lax.all_to_all(out, 'head', split_axis=0, concat_axis=1, tiled=True)  6.66 us
    all_to_all x1, starting transfers between devices, shards(): lax.all_to_all(out_grads, 'head', split_axis=1, concat_axis=0, tiled=True)  6.49 us
  transfers between devices with their start and end apart: 6, of which 3 were waited for; matrix products, arithmetic and copies ran while one was open for 7% of the time, Pallas kernels for 30%

profile of v1, /device:TPU:33, one launch (start us, length us, event | category | flops | bytes accessed | tf_op | source)
XLA Modules:
  0.0 255.9 jit_solution(10689796615765506865)
XLA Ops:
  0.6 3.4 %pad_maximum_fusion.2 = bf16[2,1536,384]{2,1,0:T(8,128)(2,1)} fusion(bf16[1,1536,384]{2,1,0:T(8,128)(2,1)} %bitcast.38, bf16[1,1536,384]{2,1,0:T(8,128)(2,1)} %bitcast.40), kind=kLoop, calls=%fused_computation.14 | loop fusion | flops 1179648 | bytes 4718592 | tf_op jit(solution)/shard_map/stack | solution.py:216
  4.0 3.7 %collective-permute-start = (bf16[2,1536,384]{2,1,0:T(8,128)(2,1)}, bf16[2,1536,384]{2,1,0:T(8,128)(2,1)}, u32[]{:S(2)}, u32[]{:S(2)}) collective-permute-start(bf16[2,1536,384]{2,1,0:T(8,128)(2,1)} %pad_maximum_fusion.2), channel_id=1, source_target_pairs={{0,8},{8,16},{16,24},{24,32},{32,40},{40,48},{48,56},{56,64},{64,7... | collective-permute-start | bytes 7077896 | tf_op jit(solution)/shard_map/ppermute | solution.py:24
  7.7 1.9 collective-permute-start.1
  9.7 1.1 copy.24
  10.8 6.5 %all-to-all-start.1 = ((bf16[192,8,384]{2,0,1:T(8,128)(2,1)}), bf16[192,8,384]{2,0,1:T(8,128)(2,1)S(1)}, u32[]{:S(2)}, u32[]{:S(2)}) async-start(bf16[192,8,384]{2,0,1:T(8,128)(2,1)} %bitcast.34), calls=%async_computation.1 | async-start | bytes 2359296 | tf_op jit(solution)/shard_map/all_to_all | solution.py:217
  18.5 0.7 gather_fusion.1
  19.5 35.9 %collective-permute-done = bf16[2,1536,384]{2,1,0:T(8,128)(2,1)} collective-permute-done((bf16[2,1536,384]{2,1,0:T(8,128)(2,1)}, bf16[2,1536,384]{2,1,0:T(8,128)(2,1)}, u32[]{:S(2)}, u32[]{:S(2)}) %collective-permute-start) | collective-permute-done | bytes 2359328 | tf_op jit(solution)/shard_map/ppermute | solution.py:24
  55.4 8.0 %collective-permute-done.1 = bf16[2,1536,384]{2,1,0:T(8,128)(2,1)} collective-permute-done((bf16[2,1536,384]{2,1,0:T(8,128)(2,1)}, bf16[2,1536,384]{2,1,0:T(8,128)(2,1)}, u32[]{:S(2)}, u32[]{:S(2)}) %collective-permute-start.1) | collective-permute-done | bytes 2359328 | tf_op jit(solution)/shard_map/ppermute | solution.py:25
  63.5 3.9 %pad_maximum_fusion = bf16[2,4608,384]{2,1,0:T(8,128)(2,1)S(1)} fusion(bf16[2,1536,384]{2,1,0:T(8,128)(2,1)} %collective-permute-done.1, bf16[1,1536,384]{2,1,0:T(8,128)(2,1)S(1)} %bitcast.39, bf16[1,1536,384]{2,1,0:T(8,128)(2,1)} %bitcast.41, bf16[2,1536,384]{2,1,0:T(8,128)(2,1)} %collective-permute-done), kind=kLoop, calls=%fused_computation.2 | loop fusion | flops 28311552 | bytes 14155776 | tf_op jit(solution)/shard_map/concatenate | solution.py:26
  67.4 3.5 %slice_bitcast_fusion = (bf16[4608,384]{1,0:T(8,128)(2,1)}, bf16[4608,384]{1,0:T(8,128)(2,1)}) fusion(bf16[2,4608,384]{2,1,0:T(8,128)(2,1)S(1)} %pad_maximum_fusion), kind=kLoop, calls=%fused_computation.7 | loop fusion | bytes 14155776 | tf_op jit(solution)/shard_map/squeeze | solution.py:222
  70.9 50.3 %shard_map.84 = (bf16[1536,384]{1,0:T(8,128)(2,1)}, f32[1536,384]{1,0:T(8,128)S(1)}) custom-call(s32[32]{0:T(128)S(1)} %reshape.35.slots_ref, s32[4]{0:T(128)S(1)} %get-tuple-element.27.counts_ref, bf16[1536,384]{1,0:T(8,128)(2,1)S(1)} %copy-done, bf16[4608,384]{1,0:T(8,128)(2,1)} %get-tuple-element.32.k_ref, bf16[4608,384]{1,0:T(8,128)(2,1)} %get-tuple-element.31.v_ref), custom_call_target="tpu_custom_call" | custom-call | tf_op jit(solution)/shard_map/pallas_call | solution.py:145
  121.3 1.4 copy-done.1
  122.7 43.8 %shard_map.85 = (f32[1536,384]{1,0:T(8,128)S(1)}, f32[3072,384]{1,0:T(8,128)}, f32[3072,384]{1,0:T(8,128)}) custom-call(s32[32]{0:T(128)S(1)} %reshape.37.slots_ref, s32[4]{0:T(128)S(1)} %get-tuple-element.25.counts_ref, bf16[1536,384]{1,0:T(8,128)(2,1)S(1)} %copy-done, bf16[1536,384]{1,0:T(8,128)(2,1)S(1)} %bitcast.35, ...), custom_call_target="tpu_custom_call" | custom-call | tf_op jit(solution)/shard_map/pallas_call | solution.py:178
  166.5 5.1 %convert_bitcast_fusion = (bf16[1,3072,384]{2,1,0:T(8,128)(2,1)S(1)}, bf16[1,3072,384]{2,1,0:T(8,128)(2,1)S(1)}) fusion(f32[3072,384]{1,0:T(8,128)} %get-tuple-element.24, f32[3072,384]{1,0:T(8,128)} %get-tuple-element.23), kind=kLoop, calls=%fused_computation.15 | loop fusion | flops 2359296 | bytes 14155776 | tf_op jit(solution)/shard_map/stack | solution.py:230
  171.6 2.4 fusion.1
  174.0 3.8 %collective-permute-start.2 = (bf16[2,1536,384]{2,1,0:T(8,128)(2,1)}, bf16[2,1536,384]{2,1,0:T(8,128)(2,1)}, u32[]{:S(2)}, u32[]{:S(2)}) collective-permute-start(bf16[2,1536,384]{2,1,0:T(8,128)(2,1)} %get-tuple-element.33), channel_id=1, source_target_pairs={{8,0},{16,8},{24,16},{32,24},{40,32},{48,40},{56,48},{64,56},{72,6... | collective-permute-start | bytes 7077896 | tf_op jit(solution)/shard_map/ppermute | solution.py:32
  177.8 1.9 collective-permute-start.3
  179.7 6.7 %all-to-all-start = ((bf16[8,192,384]{2,1,0:T(8,128)(2,1)}), bf16[8,192,384]{2,1,0:T(8,128)(2,1)S(1)}, u32[]{:S(2)}, u32[]{:S(2)}) async-start(bf16[8,192,384]{2,1,0:T(8,128)(2,1)} %bitcast.4), calls=%async_computation | async-start | bytes 2359296 | tf_op jit(solution)/shard_map/all_to_all | solution.py:223
  187.0 1.3 sort.31
  188.3 0.7 copy.14
  188.9 1.3 bitcast_or_fusion.1
  190.2 0.8 reshape.62
  191.0 1.2 gather_fusion
  192.1 0.7 reshape.65
  193.1 27.2 %shard_map.86 = (bf16[1536,384]{1,0:T(8,128)(2,1)}, f32[1536,384]{1,0:T(8,128)S(1)}, f32[1536,384]{1,0:T(8,128)}) custom-call(s32[32]{0:T(128)S(1)} %reshape.36.slots_ref, s32[4]{0:T(128)S(1)} %get-tuple-element.26.counts_ref, bf16[1536,384]{1,0:T(8,128)(2,1)S(1)} %copy-done, bf16[1536,384]{1,0:T(8,128)(2,1)S(1)} %bitcast.36, ...), custom_call_target="tpu_custom_call" | custom-call | tf_op jit(solution)/shard_map/pallas_call | solution.py:178
  220.3 1.4 copy-done.2
  221.7 25.8 %all-to-all-done = bf16[8,192,384]{2,1,0:T(8,128)(2,1)S(1)} async-done(((bf16[8,192,384]{2,1,0:T(8,128)(2,1)}), bf16[8,192,384]{2,1,0:T(8,128)(2,1)S(1)}, u32[]{:S(2)}, u32[]{:S(2)}) %all-to-all-start) | async-done | bytes 1179680 | tf_op jit(solution)/shard_map/all_to_all | solution.py:223
  247.5 1.2 copy.22
  248.7 0.9 copy-done.3
  249.6 3.9 %fusion = f32[2,1536,384]{2,1,0:T(8,128)S(1)} fusion(f32[1,1536,384]{2,1,0:T(8,128)} %bitcast.43, f32[1,1536,384]{2,1,0:T(8,128)S(1)} %bitcast.37, bf16[2,1536,384]{2,1,0:T(8,128)(2,1)} %collective-permute-done.3, bf16[2,1536,384]{2,1,0:T(8,128)(2,1)} %collective-permute-done.2), kind=kLoop, calls=%fused_computation.4 | loop fusion | flops 5898240 | bytes 14155776 | tf_op jit(solution)/shard_map/add | solution.py:239
  253.5 1.3 fusion.3
  254.8 1.1 fusion.4
  (38 shorter events, 2.4 us)
Async XLA Ops:
  0.6 9.0 %copy-start.6 = (bf16[192,3072]{1,0:T(8,128)(2,1)S(1)}, bf16[192,3072]{1,0:T(8,128)(2,1)}, u32[]{:S(2)}) copy-start(bf16[192,3072]{1,0:T(8,128)(2,1)} %param.10) | copy-start | bytes 3538948
  4.0 51.4 %collective-permute-start = (bf16[2,1536,384]{2,1,0:T(8,128)(2,1)}, bf16[2,1536,384]{2,1,0:T(8,128)(2,1)}, u32[]{:S(2)}, u32[]{:S(2)}) collective-permute-start(bf16[2,1536,384]{2,1,0:T(8,128)(2,1)} %pad_maximum_fusion.2), channel_id=1, source_target_pairs={{0,8},{8,16},{16,24},{24,32},{32,40},{40,48},{48,56},{56,64},{64,7... | collective-permute-start | bytes 7077896 | tf_op jit(solution)/shard_map/ppermute | solution.py:24
  7.7 55.8 %collective-permute-start.1 = (bf16[2,1536,384]{2,1,0:T(8,128)(2,1)}, bf16[2,1536,384]{2,1,0:T(8,128)(2,1)}, u32[]{:S(2)}, u32[]{:S(2)}) collective-permute-start(bf16[2,1536,384]{2,1,0:T(8,128)(2,1)} %pad_maximum_fusion.2), channel_id=1, source_target_pairs={{8,0},{16,8},{24,16},{32,24},{40,32},{48,40},{56,48},{64,56},{72,6... | collective-permute-start | bytes 7077896 | tf_op jit(solution)/shard_map/ppermute | solution.py:25
  9.7 7.7 %copy-start.7 = (s32[64,8]{0,1:T(8,128)S(1)}, s32[64,8]{0,1:T(8,128)}, u32[]{:S(2)}) copy-start(s32[64,8]{0,1:T(8,128)} %param.11) | copy-start | bytes 6148
  10.8 52.7 %copy-start.5 = (bf16[1536,384]{1,0:T(8,128)(2,1)S(1)}, bf16[1536,384]{1,0:T(8,128)(2,1)}, u32[]{:S(2)}) copy-start(bf16[1536,384]{1,0:T(8,128)(2,1)} %param.9) | copy-start | bytes 3538948
  10.8 111.9 %all-to-all-start.1 = ((bf16[192,8,384]{2,0,1:T(8,128)(2,1)}), bf16[192,8,384]{2,0,1:T(8,128)(2,1)S(1)}, u32[]{:S(2)}, u32[]{:S(2)}) async-start(bf16[192,8,384]{2,0,1:T(8,128)(2,1)} %bitcast.34), calls=%async_computation.1 | async-start | bytes 2359296 | tf_op jit(solution)/shard_map/all_to_all | solution.py:217
  67.4 3.6 %copy-start = (bf16[1536,384]{1,0:T(8,128)(2,1)S(1)}, bf16[1536,384]{1,0:T(8,128)(2,1)}, u32[]{:S(2)}) copy-start(bf16[1536,384]{1,0:T(8,128)(2,1)} %q_ref.5) | copy-start | bytes 3538948
  121.3 1.4 copy-start.1
  166.5 5.1 %copy-start.4 = (f32[1536,384]{1,0:T(8,128)}, f32[1536,384]{1,0:T(8,128)S(1)}, u32[]{:S(2)}) copy-start(f32[1536,384]{1,0:T(8,128)S(1)} %get-tuple-element.19.rest_0_) | copy-start | bytes 7077892
  174.0 74.7 %collective-permute-start.2 = (bf16[2,1536,384]{2,1,0:T(8,128)(2,1)}, bf16[2,1536,384]{2,1,0:T(8,128)(2,1)}, u32[]{:S(2)}, u32[]{:S(2)}) collective-permute-start(bf16[2,1536,384]{2,1,0:T(8,128)(2,1)} %get-tuple-element.33), channel_id=1, source_target_pairs={{8,0},{16,8},{24,16},{32,24},{40,32},{48,40},{56,48},{64,56},{72,6... | collective-permute-start | bytes 7077896 | tf_op jit(solution)/shard_map/ppermute | solution.py:32
  177.8 70.9 %collective-permute-start.3 = (bf16[2,1536,384]{2,1,0:T(8,128)(2,1)}, bf16[2,1536,384]{2,1,0:T(8,128)(2,1)}, u32[]{:S(2)}, u32[]{:S(2)}) collective-permute-start(bf16[2,1536,384]{2,1,0:T(8,128)(2,1)} %get-tuple-element.34), channel_id=1, source_target_pairs={{0,8},{8,16},{16,24},{24,32},{32,40},{40,48},{48,56},{56,64},{64,7... | collective-permute-start | bytes 7077896 | tf_op jit(solution)/shard_map/ppermute | solution.py:32
  179.7 67.8 %all-to-all-start = ((bf16[8,192,384]{2,1,0:T(8,128)(2,1)}), bf16[8,192,384]{2,1,0:T(8,128)(2,1)S(1)}, u32[]{:S(2)}, u32[]{:S(2)}) async-start(bf16[8,192,384]{2,1,0:T(8,128)(2,1)} %bitcast.4), calls=%async_computation | async-start | bytes 2359296 | tf_op jit(solution)/shard_map/all_to_all | solution.py:223
  220.3 1.4 copy-start.2
  247.5 2.1 copy-start.3
